TPU v7x, 256 devices: a whole 4x4x8 slice. The times are simulated.
256 devices in a mesh: row: 64 (over x, z, core), rep: 4 (over y).
Axes of the slice: x: 4, y: 4, z: 8, core: 2. Of those that a mesh axis runs over, the one named last changes fastest.
Arguments:
- features: bfloat16 [32768, 128], P(('row', 'rep')), may hold values from -6 to 6
- weight: bfloat16 [128, 256], replicated, may hold values from -0.5 to 0.5
- bias_vector: float32 [256], replicated, may hold values from -3 to 3
- cotangent: bfloat16 [32768, 256], P(('row', 'rep')), may hold values from -6 to 6
- block_tiles: bfloat16 [64, 4, 96, 1, 128, 128], P('row', 'rep'), as said below
- tile_rows: int32 [64, 4, 96, 1], P('row', 'rep'), may hold values from 0 to 3
- tile_columns: int32 [64, 4, 96, 1], P('row', 'rep'), may hold values from 0 to 63
- tile_live: int32 [64, 4, 96, 1], P('row', 'rep'), may hold values from 0 to 1, as said below
Outputs:
- activated: bfloat16 [32768, 256], P(('row', 'rep'))
- grad_features: bfloat16 [32768, 128], P(('row', 'rep'))
- grad_weight: float32 [128, 256], replicated
- grad_bias: float32 [256], replicated
Inputs may be any that keep to these rules, and one draw needn't show every extreme that they name: `block_tiles`: A is symmetric: the tile that a live slot puts at block (i, j) is the transpose of the tile that a live slot puts at block (j, i); every block row has a live diagonal tile. `tile_live`: the number of live slots differs from device to device.
All inputs are finite; a program needn't handle non-finite values.
Results may differ from a plain program's by a relative error of at most 0.0095.
Values may be sent and summed in bfloat16 or wider, within the bound.
No kernel may reach another device: no remote copies, remote signals or barrier semaphores. Data moves between devices by JAX's collectives and lax.ppermute only.
A program may use at most 64 MiB of HBM per device.

v0:
```python
import math

import jax
import jax.numpy as jnp
from jax import lax
from jax.sharding import PartitionSpec as P


def aggregate(panel, block_tiles, tile_rows, tile_columns, tile_live, group_rows):
    tile_size = block_tiles.shape[-1]
    feat_width = panel.shape[1]
    slot_count = block_tiles.shape[2] * block_tiles.shape[3]
    tile_list = block_tiles.reshape(slot_count, tile_size, tile_size)
    row_list = tile_rows.reshape(slot_count)
    column_list = tile_columns.reshape(slot_count)
    live_list = tile_live.reshape(slot_count)
    split_panel = panel.dtype != jnp.bfloat16
    high_part = panel.astype(jnp.bfloat16)
    low_part = (panel - high_part.astype(jnp.float32)).astype(jnp.bfloat16)
    high_blocks = high_part.reshape(-1, tile_size, feat_width)
    low_blocks = low_part.reshape(-1, tile_size, feat_width)
    ranking = jnp.argsort(1 - live_list, stable=True)
    live_count = jnp.sum(live_list)
    stride = math.gcd(slot_count, 8)
    turn_count = (live_count + stride - 1) // stride
    targets = jnp.arange(group_rows, dtype=jnp.int32)

    def visit(turn_index, running):
        chosen = lax.dynamic_slice_in_dim(ranking, turn_index * stride, stride)
        tile_part = tile_list[chosen]
        picked_columns = column_list[chosen]
        products = jnp.einsum(
            "sij,sjw->siw",
            tile_part,
            high_blocks[picked_columns],
            preferred_element_type=jnp.float32,
        )
        products = products + jnp.einsum(
            "sij,sjw->siw",
            tile_part,
            low_blocks[picked_columns],
            preferred_element_type=jnp.float32,
        )
        placing = (row_list[chosen][:, None] == targets[None, :]).astype(jnp.float32)
        placing = placing * live_list[chosen][:, None].astype(jnp.float32)
        return running + jnp.einsum(
            "sg,siw->giw", placing, products, precision=lax.Precision.HIGHEST
        )

    running = lax.fori_loop(
        0, turn_count, visit, jnp.zeros((group_rows, tile_size, feat_width), jnp.float32)
    )
    return running.reshape(group_rows * tile_size, feat_width)


def activate(values):
    return jax.nn.gelu(values, approximate=True)


def shards(
    features, weight, bias_vector, cotangent, block_tiles, tile_rows, tile_columns, tile_live
):
    tile_size = block_tiles.shape[-1]
    group_rows = lax.axis_size("rep") * (features.shape[0] // tile_size)
    node_total = features.shape[0] * lax.axis_size("row") * lax.axis_size("rep")
    weight_wide = weight.astype(jnp.float32)
    projected = jnp.dot(features, weight, preferred_element_type=jnp.float32)
    input_panel = lax.all_gather(projected, "row", axis=0, tiled=True)
    partial_rows = aggregate(
        input_panel, block_tiles, tile_rows, tile_columns, tile_live, group_rows
    )
    hidden = lax.psum_scatter(partial_rows, "rep", scatter_dimension=0, tiled=True) + bias_vector
    activated, pullback = jax.vjp(activate, hidden)
    grad_hidden = pullback(cotangent.astype(jnp.float32))[0]
    grad_panel = lax.all_gather(grad_hidden, "row", axis=0, tiled=True)
    grad_rows = aggregate(grad_panel, block_tiles, tile_rows, tile_columns, tile_live, group_rows)
    spread = lax.psum_scatter(grad_rows, "rep", scatter_dimension=0, tiled=True)
    grad_features = jnp.dot(
        spread, weight_wide.T, precision=lax.Precision.HIGHEST, preferred_element_type=jnp.float32
    ).astype(jnp.bfloat16)
    weight_term = jnp.dot(
        features.astype(jnp.float32).T,
        spread,
        precision=lax.Precision.HIGHEST,
        preferred_element_type=jnp.float32,
    )
    grad_weight, grad_bias = lax.psum((weight_term, jnp.sum(grad_hidden, axis=0)), ("row", "rep"))
    factor = 1.0 / math.sqrt(node_total)
    return (activated.astype(jnp.bfloat16), grad_features, grad_weight * factor, grad_bias * factor)


def solution(mesh):
    in_specs = (
        P(("row", "rep"), None),
        P(),
        P(),
        P(("row", "rep"), None),
        P("row", "rep", None, None, None, None),
        P("row", "rep", None, None),
        P("row", "rep", None, None),
        P("row", "rep", None, None),
    )
    out_specs = (P(("row", "rep"), None), P(("row", "rep"), None), P(), P())
    return jax.shard_map(shards, mesh=mesh, in_specs=in_specs, out_specs=out_specs, check_vma=False)
```

profile of v0, /device:TPU:1, one launch (start us, length us, event | category | flops | bytes accessed | tf_op | source)
XLA Modules:
  0.0 884.6 jit_solution(16110552708149175523)
XLA Ops:
  12.3 2.6 sort.19
  14.9 83.7 %all-gather.3.cloned.1.call-done = f32[8192,256]{1,0:T(8,128)} async-done(((f32[128,256]{1,0:T(8,128)}), f32[8192,256]{1,0:T(8,128)}) %all-gather.3.cloned.1.call-update) | async-done | bytes 8388624 | tf_op jit(solution)/shard_map/all_gather | solution.py:68
  98.5 10.5 %subtract_convert_fusion.1 = (bf16[8192,256]{1,0:T(8,128)(2,1)}, bf16[8192,256]{1,0:T(8,128)(2,1)}) fusion(f32[8192,256]{1,0:T(8,128)} %all-gather.3.cloned.1.call-done), kind=kLoop, calls=%fused_computation.45 | loop fusion | flops 8388608 | bytes 16777216 | tf_op jit(solution)/shard_map/convert_element_type | solution.py:19
  109.2 111.4 %while.22 = (s32[]{:T(128)}, f32[4,128,256]{2,0,1:T(4,128)S(1)}, s32[]{:T(128)}, s32[96]{0:T(128)}, s32[96]{0:T(128)S(1)}, /*index=5*/s32[96]{0:T(128)S(1)}, bf1...) while((s32[]{:T(128)}, f32[4,128,256]{2,0,1:T(4,128)S(1)}, ...), condition=%wide.region_3.4_spmd.clone, body=%wide.region_2.3_spmd.clone.sunk | while | flops 147196032 | bytes 9446263 | solution.py:50
  110.6 2.8 gather_fusion.3
  113.4 2.5 gather_fusion
  116.1 2.8 gather_fusion.2
  120.5 2.6 convolution_add_fusion.4
  124.5 2.8 gather_fusion.3
  127.3 2.5 gather_fusion
  130.1 2.8 gather_fusion.2
  134.4 2.6 convolution_add_fusion.4
  138.4 2.8 gather_fusion.3
  141.2 2.5 gather_fusion
  144.0 2.8 gather_fusion.2
  148.4 2.6 convolution_add_fusion.4
  152.4 2.8 gather_fusion.3
  155.1 2.5 gather_fusion
  157.9 2.8 gather_fusion.2
  162.3 2.6 convolution_add_fusion.4
  166.3 2.8 gather_fusion.3
  169.1 2.5 gather_fusion
  171.9 2.8 gather_fusion.2
  176.2 2.6 convolution_add_fusion.4
  180.2 2.8 gather_fusion.3
  185.8 2.8 gather_fusion.2
  190.1 2.6 convolution_add_fusion.4
  194.2 2.8 gather_fusion.3
  199.7 2.8 gather_fusion.2
  204.1 2.6 convolution_add_fusion.4
  208.1 2.8 gather_fusion.3
  213.6 2.8 gather_fusion.2
  218.0 2.6 convolution_add_fusion.4
  221.6 72.1 %reduce-scatter.3.cloned.1.call-done = f32[128,256]{1,0:T(8,128)} async-done(((f32[512,256]{1,0:T(8,128)}), f32[128,256]{1,0:T(8,128)}) %reduce-scatter.3.cloned.1.call-update) | async-done | bytes 131088 | tf_op jit(solution)/shard_map/reduce_scatter | solution.py:72
  296.0 86.5 %all-gather.5.cloned.1.call-done = f32[8192,256]{1,0:T(8,128)} async-done(((f32[128,256]{1,0:T(8,128)}), f32[8192,256]{1,0:T(8,128)}) %all-gather.5.cloned.1.call-update) | async-done | bytes 8388624 | tf_op jit(solution)/shard_map/all_gather | solution.py:75
  382.5 10.5 %subtract_convert_fusion = (bf16[8192,256]{1,0:T(8,128)(2,1)}, bf16[8192,256]{1,0:T(8,128)(2,1)}) fusion(f32[8192,256]{1,0:T(8,128)} %all-gather.5.cloned.1.call-done), kind=kLoop, calls=%fused_computation.44 | loop fusion | flops 8388608 | bytes 16777216 | tf_op jit(solution)/shard_map/convert_element_type | solution.py:19
  393.1 111.4 %while.23 = (s32[]{:T(128)}, f32[4,128,256]{2,0,1:T(4,128)S(1)}, s32[]{:T(128)}, s32[96]{0:T(128)}, s32[96]{0:T(128)S(1)}, /*index=5*/s32[96]{0:T(128)S(1)}, bf1...) while((s32[]{:T(128)}, f32[4,128,256]{2,0,1:T(4,128)S(1)}, ...), condition=%wide.region_6.7_spmd.clone, body=%wide.region_5.6_spmd.clone.sunk | while | flops 147196032 | bytes 9446263 | solution.py:50
  394.6 2.8 gather_fusion.9
  400.1 2.8 gather_fusion.8
  404.5 2.6 convolution_add_fusion.5
  408.5 2.8 gather_fusion.9
  414.0 2.8 gather_fusion.8
  418.4 2.6 convolution_add_fusion.5
  422.4 2.8 gather_fusion.9
  428.0 2.8 gather_fusion.8
  432.3 2.6 convolution_add_fusion.5
  436.3 2.8 gather_fusion.9
  441.9 2.8 gather_fusion.8
  446.3 2.6 convolution_add_fusion.5
  450.3 2.8 gather_fusion.9
  453.0 2.5 gather_fusion.6
  455.8 2.8 gather_fusion.8
  460.2 2.6 convolution_add_fusion.5
  464.2 2.8 gather_fusion.9
  469.8 2.8 gather_fusion.8
  474.1 2.6 convolution_add_fusion.5
  478.1 2.8 gather_fusion.9
  483.7 2.8 gather_fusion.8
  488.0 2.6 convolution_add_fusion.5
  492.1 2.8 gather_fusion.9
  497.6 2.8 gather_fusion.8
  502.0 2.6 convolution_add_fusion.5
  505.6 129.4 %psum.15 = f32[256]{0:T(256)S(1)} all-reduce(f32[256]{0:T(256)S(1)} %copy-done.6), channel_id=1, replica_groups=mesh['row'=64,'rep'=4] {'row','rep'}, use_global_device_ids=true, to_apply=%region_10.11 | all-reduce | flops 256 | bytes 2048 | tf_op jit(solution)/shard_map/psum | solution.py:87
  639.1 237.3 %all-reduce.2.cloned.1.call-done = f32[128,256]{0,1:T(8,128)} async-done(((f32[128,256]{0,1:T(8,128)}), f32[128,256]{0,1:T(8,128)}) %all-reduce.2.cloned.1.call-update) | async-done | bytes 131088 | tf_op jit(solution)/shard_map/psum | solution.py:87
  (209 shorter events, 91.4 us)
Async XLA Ops:
  7.2 0.8 copy-start
  7.2 91.3 %all-gather.3.cloned.1.call-start = ((), (), s32[]{:S(2)}) async-start(), calls=%async_computation.2 | async-start | bytes 8519680 | tf_op jit(solution)/shard_map/all_gather | solution.py:68
  9.6 284.1 %reduce-scatter.3.cloned.1.call-start = ((), (), s32[]{:S(2)}) async-start(), calls=%async_computation.3 | async-start | bytes 655360 | tf_op jit(solution)/shard_map/reduce_scatter | solution.py:72
  14.9 94.3 %copy-start.1 = (s32[1,1,96,1]{2,3,1,0:T(1,128)S(1)}, s32[1,1,96,1]{2,3,1,0:T(1,128)}, u32[]{:S(2)}) copy-start(s32[1,1,96,1]{2,3,1,0:T(1,128)} %param.19) | copy-start | bytes 1156
  14.9 94.3 %copy-start.2 = (s32[1,1,96,1]{2,3,1,0:T(1,128)S(1)}, s32[1,1,96,1]{2,3,1,0:T(1,128)}, u32[]{:S(2)}) copy-start(s32[1,1,96,1]{2,3,1,0:T(1,128)} %param.17) | copy-start | bytes 1156
  14.9 94.3 %copy-start.3 = (s32[1,1,96,1]{2,3,1,0:T(1,128)S(1)}, s32[1,1,96,1]{2,3,1,0:T(1,128)}, u32[]{:S(2)}) copy-start(s32[1,1,96,1]{2,3,1,0:T(1,128)} %param.18) | copy-start | bytes 1156
  109.2 184.5 %copy-start.5 = (bf16[128,256]{1,0:T(8,128)(2,1)S(1)}, bf16[128,256]{1,0:T(8,128)(2,1)}, u32[]{:S(2)}) copy-start(bf16[128,256]{1,0:T(8,128)(2,1)} %param.15) | copy-start | bytes 196612
  221.5 161.0 %all-gather.5.cloned.1.call-start = ((), (), s32[]{:S(2)}) async-start(), calls=%async_computation.4 | async-start | bytes 8519680 | tf_op jit(solution)/shard_map/all_gather | solution.py:75
  295.9 339.5 %reduce-scatter.5.cloned.1.call-start = ((), (), s32[]{:S(2)}) async-start(), calls=%async_computation.5 | async-start | bytes 655360 | tf_op jit(solution)/shard_map/reduce_scatter | solution.py:77
  393.1 112.4 %copy-start.6 = (f32[256]{0:T(256)S(1)}, f32[256]{0:T(256)}, u32[]{:S(2)}) copy-start(f32[256]{0:T(256)} %get-tuple-element.218) | copy-start | bytes 3076
  393.1 242.4 %copy-start.4 = (bf16[128,128]{1,0:T(8,128)(2,1)S(1)}, bf16[128,128]{1,0:T(8,128)(2,1)}, u32[]{:S(2)}) copy-start(bf16[128,128]{1,0:T(8,128)(2,1)} %param.12) | copy-start | bytes 98308
  505.5 370.9 %all-reduce.2.cloned.1.call-start = ((), (), s32[]{:S(2)}) async-start(), calls=%async_computation.6 | async-start | bytes 262144 | tf_op jit(solution)/shard_map/psum | solution.py:87
Sparse Core Ops, SparseCore 0:
  11.3 87.1 all-gather.2
  221.6 71.9 reduce-scatter.2
  297.0 85.4 all-gather.4
  505.6 71.9 reduce-scatter.4
  637.5 238.9 all-reduce.1
where the time goes:
time: 888 us; the launch traced here: 885 us
  waiting for transfers between devices  480 us (54%)
  local copies, waits for them, and re-layouts  163 us (18%)
  blocking collectives  129 us (15%)
  matrix products  55.9 us (6%)
  other arithmetic  41.3 us (5%)
  between operations  14.5 us (2%)
    psum x1, waiting for transfers between devices, shards(): lax.psum((weight_term, jnp.sum(grad_hidden, axis=0)), ('row', 'rep'))  237 us
    psum x1, blocking collectives, shards(): lax.psum((weight_term, jnp.sum(grad_hidden, axis=0)), ('row', 'rep'))  129 us
    all_gather x1, waiting for transfers between devices, shards(): grad_panel = lax.all_gather(grad_hidden, 'row', axis=0, tiled=True)  86.5 us
    all_gather x1, waiting for transfers between devices, shards(): input_panel = lax.all_gather(projected, 'row', axis=0, tiled=True)  83.7 us
    reduce_scatter x1, waiting for transfers between devices, shards(): lax.psum_scatter(partial_rows, 'rep', scatter_dimension=0, tiled=True)  72.1 us
    gather x16, local copies, waits for them, and re-layouts, visit(): high_blocks[picked_columns]  44.3 us
    gather x16, local copies, waits for them, and re-layouts, visit(): low_blocks[picked_columns]  44.3 us
    dot_general x16, matrix products, visit(): jnp.einsum('sg,siw->giw', placing, products, precision=lax.Precision.HIGH...  41.7 us
  transfers between devices with their start and end apart: 5, of which 4 were waited for; matrix products, arithmetic and copies ran while one was open for 1% of the time, Pallas kernels for 0%

commit v1 on v0

v1 whole, which is shorter than its diff:
```python
import math

import jax
import jax.numpy as jnp
from jax import lax
from jax.experimental import pallas as pl
from jax.experimental.pallas import tpu as pltpu
from jax.sharding import PartitionSpec as P

SLOT_CHUNK = 16


def _agg_kernel(cols_ref, rows_ref, live_ref, tiles_ref, *rest):
    *panel_refs, out_ref = rest
    step = pl.program_id(0)
    chunk = tiles_ref.shape[0]

    @pl.when(step == 0)
    def _():
        out_ref[...] = jnp.zeros_like(out_ref)

    for k in range(chunk):
        slot = step * chunk + k
        column = cols_ref[slot]
        row = rows_ref[slot]

        @pl.when(live_ref[slot] != 0)
        def _():
            tile = tiles_ref[k]
            acc = jnp.dot(tile, panel_refs[0][column], preferred_element_type=jnp.float32)
            for panel_ref in panel_refs[1:]:
                acc = acc + jnp.dot(tile, panel_ref[column], preferred_element_type=jnp.float32)
            out_ref[row] += acc


def aggregate(tiles, cols, rows, live, panels, group_rows):
    slot_count, tile_size, _ = tiles.shape
    n_blocks, _, width = panels[0].shape
    chunk = math.gcd(slot_count, SLOT_CHUNK)
    grid_spec = pltpu.PrefetchScalarGridSpec(
        num_scalar_prefetch=3,
        grid=(slot_count // chunk,),
        in_specs=[pl.BlockSpec((chunk, tile_size, tile_size), lambda i, *_: (i, 0, 0))]
        + [pl.BlockSpec((n_blocks, tile_size, width), lambda i, *_: (0, 0, 0)) for _ in panels],
        out_specs=pl.BlockSpec((group_rows, tile_size, width), lambda i, *_: (0, 0, 0)),
    )
    return pl.pallas_call(
        _agg_kernel,
        grid_spec=grid_spec,
        out_shape=jax.ShapeDtypeStruct((group_rows, tile_size, width), jnp.float32),
        compiler_params=pltpu.CompilerParams(dimension_semantics=("arbitrary",)),
    )(cols, rows, live, tiles, *panels)


def gather_rows_a2a(block, axis):
    n = lax.axis_size(axis)
    spread = jnp.broadcast_to(block[None], (n,) + block.shape)
    return lax.all_to_all(spread, axis, 0, 0, tiled=False)


def reduce_rep_a2a(parts):
    received = lax.all_to_all(parts, "rep", 0, 0, tiled=False)
    total = received[0]
    for j in range(1, received.shape[0]):
        total = total + received[j]
    return total


def activate(values):
    return jax.nn.gelu(values, approximate=True)


def split_bf16(values):
    high = values.astype(jnp.bfloat16)
    low = (values - high.astype(jnp.float32)).astype(jnp.bfloat16)
    return high, low


def shards(
    features, weight, bias_vector, cotangent, block_tiles, tile_rows, tile_columns, tile_live
):
    tile_size = block_tiles.shape[-1]
    n_rep = lax.axis_size("rep")
    n_row = lax.axis_size("row")
    fin = features.shape[1]
    fout = weight.shape[1]
    node_total = features.shape[0] * n_row * n_rep
    group_rows = n_rep * (features.shape[0] // tile_size)
    slot_count = block_tiles.shape[2] * block_tiles.shape[3]
    tiles = block_tiles.reshape(slot_count, tile_size, tile_size)
    rows = tile_rows.reshape(slot_count)
    cols = tile_columns.reshape(slot_count)
    live = tile_live.reshape(slot_count)
    weight_wide = weight.astype(jnp.float32)

    x_panel = gather_rows_a2a(features.reshape(-1, tile_size, fin), "row")
    x_panel = x_panel.reshape(n_row, tile_size, fin)
    z_parts = aggregate(tiles, cols, rows, live, [x_panel], group_rows)
    z_own = reduce_rep_a2a(z_parts.reshape(n_rep, -1, fin)).reshape(-1, fin)
    hidden = (
        jnp.dot(z_own, weight_wide, precision=lax.Precision.HIGHEST, preferred_element_type=jnp.float32)
        + bias_vector
    )
    activated, pullback = jax.vjp(activate, hidden)
    grad_hidden = pullback(cotangent.astype(jnp.float32))[0]

    joined = jnp.concatenate([z_own, grad_hidden], axis=1)
    joined_all = lax.all_gather(joined, "row", axis=0, tiled=True)
    z_quarter = joined_all[:, :fin]
    dh_quarter = joined_all[:, fin:]
    p_quarter = jnp.dot(
        dh_quarter, weight_wide.T, precision=lax.Precision.HIGHEST, preferred_element_type=jnp.float32
    )
    p_high, p_low = split_bf16(p_quarter.reshape(n_row, tile_size, fin))
    g_parts = aggregate(tiles, cols, rows, live, [p_high, p_low], group_rows)
    grad_features = reduce_rep_a2a(g_parts.reshape(n_rep, -1, fin)).reshape(-1, fin)

    weight_term = lax.dot_general(
        z_quarter,
        dh_quarter,
        (((0,), (0,)), ((), ())),
        precision=lax.Precision.HIGHEST,
        preferred_element_type=jnp.float32,
    )
    bias_term = jnp.sum(dh_quarter, axis=0)
    pad = (-(fin + 1)) % 8
    terms = jnp.concatenate(
        [weight_term, bias_term[None], jnp.zeros((pad, fout), jnp.float32)], axis=0
    )
    spread = jnp.broadcast_to(terms[None], (n_rep,) + terms.shape)
    totals = reduce_rep_a2a(spread)
    factor = 1.0 / math.sqrt(node_total)
    grad_weight = totals[:fin] * factor
    grad_bias = totals[fin] * factor
    return (activated.astype(jnp.bfloat16), grad_features.astype(jnp.bfloat16), grad_weight, grad_bias)


def solution(mesh):
    in_specs = (
        P(("row", "rep"), None),
        P(),
        P(),
        P(("row", "rep"), None),
        P("row", "rep", None, None, None, None),
        P("row", "rep", None, None),
        P("row", "rep", None, None),
        P("row", "rep", None, None),
    )
    out_specs = (P(("row", "rep"), None), P(("row", "rep"), None), P(), P())
    return jax.shard_map(shards, mesh=mesh, in_specs=in_specs, out_specs=out_specs, check_vma=False)
```

time: 888 us -> 254 us (0.29)
  waiting for transfers between devices: 480 us -> 97.8 us
  local copies, waits for them, and re-layouts: 163 us -> 2.18 us
  blocking collectives: 129 us -> 74.7 us
  matrix products: 55.9 us -> 18.7 us
  other arithmetic: 41.3 us -> 10.4 us
  Pallas kernels: 0 us -> 23.5 us
    psum x1 -> x0, waiting for transfers between devices: 237 us -> none  [shards(): lax.psum((weight_term, jnp.sum(grad_hidden, axis=0)), ('row', 'rep'))]
    gather x96 -> x0, local copies, waits for them, and re-layouts: 159 us -> none  [the longest x16 44.3 us: visit(): high_blocks[picked_columns]]
    psum x1 -> x0, blocking collectives: 129 us -> none  [shards(): lax.psum((weight_term, jnp.sum(grad_hidden, axis=0)), ('row', 'rep'))]
    all_gather x2 -> x1, waiting for transfers between devices: 170 us -> 90 us  [shards(): joined_all = lax.all_gather(joined, 'row', axis=0, tiled=True)]
    all_to_all x0 -> x2, blocking collectives: none -> 74.7 us  [the longest x1 64.1 us: gather_rows_a2a(): return lax.all_to_all(spread, axis, 0, 0, tiled=False)]
    reduce_scatter x2 -> x0, waiting for transfers between devices: 72.1 us -> none  [the longest x1 72.1 us: shards(): lax.psum_scatter(partial_rows, 'rep', scatter_dimension=0, tiled=True)]
    dot_general x51 -> x3, matrix products: 55.9 us -> 18.7 us  [the longest x1 11.5 us: shards(): lax.dot_general(z_quarter, dh_quarter, (((0,), (0,)), ((), ())), precisio...]
    pallas_call x0 -> x2, Pallas kernels: none -> 23.5 us  [aggregate(): pl.pallas_call(_agg_kernel, grid_spec=grid_spec, out_shape=jax.ShapeDtype...]
  transfers between devices with their start and end apart: 5 -> 3, of which waited for: 4 -> 2; matrix products, arithmetic and copies ran while one was open for 1% -> 7% of each run, Pallas kernels for 0% -> 0%
where the time goes in v1:
time: 254 us; the launch traced here: 250 us
  waiting for transfers between devices  97.8 us (39%)
  blocking collectives  74.7 us (29%)
  Pallas kernels  23.5 us (9%)
  matrix products  18.7 us (7%)
  between operations  14.1 us (6%)
  other arithmetic  10.4 us (4%)
  starting transfers between devices  8.91 us (4%)
    all_gather x1, waiting for transfers between devices, shards(): joined_all = lax.all_gather(joined, 'row', axis=0, tiled=True)  90 us
    all_to_all x1, blocking collectives, gather_rows_a2a(): return lax.all_to_all(spread, axis, 0, 0, tiled=False)  64.1 us
    pallas_call x2, Pallas kernels, aggregate(): pl.pallas_call(_agg_kernel, grid_spec=grid_spec, out_shape=jax.ShapeDtype...  23.5 us
    dot_general x1, matrix products, shards(): lax.dot_general(z_quarter, dh_quarter, (((0,), (0,)), ((), ())), precisio...  11.5 us
    all_to_all x1, blocking collectives, reduce_rep_a2a(): received = lax.all_to_all(parts, 'rep', 0, 0, tiled=False)  10.6 us
    all_to_all x2, starting transfers between devices, reduce_rep_a2a(): received = lax.all_to_all(parts, 'rep', 0, 0, tiled=False)  8.87 us
    all_to_all x2, waiting for transfers between devices, reduce_rep_a2a(): received = lax.all_to_all(parts, 'rep', 0, 0, tiled=False)  7.77 us
    dot_general x1, matrix products, shards(): jnp.dot(dh_quarter, weight_wide.T, precision=lax.Precision.HIGHEST, prefe...  6.28 us
  transfers between devices with their start and end apart: 3, of which 2 were waited for; matrix products, arithmetic and copies ran while one was open for 7% of the time, Pallas kernels for 0%

profile of v1, /device:TPU:1, one launch (start us, length us, event | category | flops | bytes accessed | tf_op | source)
XLA Modules:
  0.0 250.3 jit_solution(15060314954743770693)
XLA Ops:
  7.2 0.0 copy-start
  7.2 0.0 all-gather.2.cloned.1.call-start
  7.2 1.3 broadcast_in_dim.8
  8.5 64.1 %all_to_all.20 = bf16[64,1,128,128]{3,2,1,0:T(8,128)(2,1)} all-to-all(bf16[64,1,128,128]{3,2,1,0:T(8,128)(2,1)S(1)} %broadcast_in_dim.8), channel_id=1, replica_groups=mesh['row'=64,'rep'=4] {'row'}, dimensions={0} | all-to-all | bytes 4194304 | tf_op jit(solution)/shard_map/all_to_all | solution.py:58
  72.6 0.0 copy-start.1
  72.6 0.0 copy-start.2
  72.6 10.9 %shard_map.111 = f32[4,128,128]{2,1,0:T(8,128)} custom-call(s32[96]{0:T(128)} %bitcast.22, s32[96]{0:T(128)} %bitcast.24, s32[96]{0:T(128)} %bitcast.26, bf16[96,128,128]{2,1,0:T(8,128)(2,1)} %bitcast.18, bf16[64,128,128]{2,1,0:T(8,128)(2,1)} %bitcast.20), custom_call_target="tpu_custom_call" | custom-call | tf_op jit(solution)/shard_map/pallas_call | solution.py:47
  83.5 10.6 %all_to_all.21 = f32[4,128,128]{2,1,0:T(8,128)S(1)} all-to-all(f32[4,128,128]{2,1,0:T(8,128)} %shard_map.111), channel_id=1, replica_groups=mesh['row'=64,'rep'=4] {'rep'}, dimensions={0} | all-to-all | bytes 524288 | tf_op jit(solution)/shard_map/all_to_all | solution.py:62
  94.1 0.0 copy-done
  94.1 0.0 copy-done.1
  94.1 0.0 copy-done.2
  94.1 0.9 fusion.6
  95.0 0.7 pad_maximum_fusion
  95.7 0.0 all-gather.2.cloned.1.call-update
  95.8 0.1 pad.2.clone
  95.8 90.0 %all-gather.2.cloned.1.call-done = f32[8192,384]{1,0:T(8,128)} async-done(((f32[128,384]{1,0:T(8,128)}), f32[8192,384]{1,0:T(8,128)}) %all-gather.2.cloned.1.call-update) | async-done | bytes 12582928 | tf_op jit(solution)/shard_map/all_gather | solution.py:108
  185.8 6.3 %fusion.2 = f32[8192,128]{1,0:T(8,128)S(1)} fusion(bf16[128,256]{1,0:T(8,128)(2,1)S(1)} %copy-done, f32[8192,384]{1,0:T(8,128)} %all-gather.2.cloned.1.call-done), kind=kOutput, calls=%fused_computation.3 | convolution fusion | flops 3221225472 | bytes 12648448 | tf_op jit(solution)/shard_map/dot_general | solution.py:111
  192.1 3.1 %subtract_convert_fusion = (bf16[64,128,128]{2,1,0:T(8,128)(2,1)}, bf16[64,128,128]{2,1,0:T(8,128)(2,1)}) fusion(f32[64,128,128]{2,1,0:T(8,128)S(1)} %bitcast.17), kind=kLoop, calls=%fused_computation.6 | loop fusion | flops 4194304 | bytes 8388608 | tf_op jit(solution)/shard_map/convert_element_type | solution.py:75
  195.2 12.6 %shard_map.112 = f32[4,128,128]{2,1,0:T(8,128)} custom-call(s32[96]{0:T(128)} %bitcast.23, s32[96]{0:T(128)} %bitcast.25, s32[96]{0:T(128)} %bitcast.27, bf16[96,128,128]{2,1,0:T(8,128)(2,1)} %bitcast.19, bf16[64,128,128]{2,1,0:T(8,128)(2,1)} %get-tuple-element.5.rest_0_, bf16[64,128,128]{2,1,0:T(8,128)(2,1)} %get-tuple-element.4.rest_1_), custom_call_target="tpu_custom_call" | custom-call | tf_op jit(solution)/shard_map/pallas_call | solution.py:47
  207.8 4.6 %all-to-all-start.2 = ((f32[4,128,128]{2,1,0:T(8,128)}), f32[4,128,128]{2,1,0:T(8,128)S(1)}, u32[]{:S(2)}, u32[]{:S(2)}) async-start(f32[4,128,128]{2,1,0:T(8,128)} %shard_map.112), calls=%async_computation.2 | async-start | bytes 524288 | tf_op jit(solution)/shard_map/all_to_all | solution.py:62
  212.4 4.6 %slice_reduce_fusion = f32[256]{0:T(256)S(1)} fusion(f32[8192,384]{1,0:T(8,128)} %all-gather.2.cloned.1.call-done), kind=kLoop, calls=%fused_computation | loop fusion | flops 2096896 | bytes 8389632 | tf_op jit(solution)/shard_map/reduce_sum | solution.py:125
  217.0 11.5 %fusion = f32[128,256]{1,0:T(8,128)S(1)} fusion(f32[8192,384]{1,0:T(8,128)} %all-gather.2.cloned.1.call-done), kind=kOutput, calls=%fused_computation.1 | convolution fusion | flops 3221225472 | bytes 12713984 | tf_op jit(solution)/shard_map/dot_general | solution.py:118
  228.6 0.1 maximum_maximum_fusion
  228.7 0.0 all-to-all-done.2
  228.7 0.8 broadcast_in_dim.21
  229.5 4.2 %all-to-all-start.3 = ((f32[4,136,256]{2,1,0:T(8,128)}), f32[4,136,256]{2,1,0:T(8,128)S(1)}, u32[]{:S(2)}, u32[]{:S(2)}) async-start(f32[4,136,256]{2,1,0:T(8,128)} %broadcast_in_dim.21), calls=%async_computation.3 | async-start | bytes 1114112 | tf_op jit(solution)/shard_map/all_to_all | solution.py:62
  233.7 0.6 fusion.17
  234.4 7.8 %all-to-all-done.3 = f32[4,136,256]{2,1,0:T(8,128)S(1)} async-done(((f32[4,136,256]{2,1,0:T(8,128)}), f32[4,136,256]{2,1,0:T(8,128)S(1)}, u32[]{:S(2)}, u32[]{:S(2)}) %all-to-all-start.3) | async-done | bytes 557088 | tf_op jit(solution)/shard_map/all_to_all | solution.py:62
  242.2 0.6 slice_multiply_fusion.1
  242.7 0.7 fusion.14
  (3 shorter events, 0.1 us)
Async XLA Ops:
  7.2 86.9 %copy-start = (bf16[128,256]{1,0:T(8,128)(2,1)S(1)}, bf16[128,256]{1,0:T(8,128)(2,1)}, u32[]{:S(2)}) copy-start(bf16[128,256]{1,0:T(8,128)(2,1)} %param.9) | copy-start | bytes 196612
  7.2 178.7 %all-gather.2.cloned.1.call-start = ((), (), s32[]{:S(2)}) async-start(), calls=%async_computation.4 | async-start | bytes 12779520 | tf_op jit(solution)/shard_map/all_gather | solution.py:108
  72.6 21.5 %copy-start.1 = (bf16[128,256]{1,0:T(8,128)(2,1)S(1)}, bf16[128,256]{1,0:T(8,128)(2,1)}, u32[]{:S(2)}) copy-start(bf16[128,256]{1,0:T(8,128)(2,1)} %param.11) | copy-start | bytes 196612
  72.6 21.5 %copy-start.2 = (f32[256]{0:T(256)S(1)}, f32[256]{0:T(256)}, u32[]{:S(2)}) copy-start(f32[256]{0:T(256)} %param.10) | copy-start | bytes 3076
  207.8 20.9 %all-to-all-start.2 = ((f32[4,128,128]{2,1,0:T(8,128)}), f32[4,128,128]{2,1,0:T(8,128)S(1)}, u32[]{:S(2)}, u32[]{:S(2)}) async-start(f32[4,128,128]{2,1,0:T(8,128)} %shard_map.112), calls=%async_computation.2 | async-start | bytes 524288 | tf_op jit(solution)/shard_map/all_to_all | solution.py:62
  229.5 12.6 %all-to-all-start.3 = ((f32[4,136,256]{2,1,0:T(8,128)}), f32[4,136,256]{2,1,0:T(8,128)S(1)}, u32[]{:S(2)}, u32[]{:S(2)}) async-start(f32[4,136,256]{2,1,0:T(8,128)} %broadcast_in_dim.21), calls=%async_computation.3 | async-start | bytes 1114112 | tf_op jit(solution)/shard_map/all_to_all | solution.py:62
Sparse Core Ops, SparseCore 0:
  95.9 89.9 all-gather.1

commit v2 on v1

--- a/solution.py
+++ b/solution.py
@@ -5,7 +5,7 @@
 from jax import lax
 from jax.experimental import pallas as pl
 from jax.experimental.pallas import tpu as pltpu
-from jax.sharding import PartitionSpec as P
+from jax.sharding import Mesh, PartitionSpec as P
 
 SLOT_CHUNK = 16
 
@@ -52,10 +52,24 @@
     )(cols, rows, live, tiles, *panels)
 
 
-def gather_rows_a2a(block, axis):
+def gather_a2a(block, axis):
     n = lax.axis_size(axis)
     spread = jnp.broadcast_to(block[None], (n,) + block.shape)
     return lax.all_to_all(spread, axis, 0, 0, tiled=False)
+
+
+def gather_rows(block):
+    return gather_a2a(gather_a2a(gather_a2a(block, "z"), "x"), "core")
+
+
+def panel_index(cols):
+    n_z = lax.axis_size("z")
+    n_core = lax.axis_size("core")
+    n_x = lax.axis_size("x")
+    core = cols % n_core
+    z = (cols // n_core) % n_z
+    x = cols // (n_core * n_z)
+    return (core * n_x + x) * n_z + z
 
 
 def reduce_rep_a2a(parts):
@@ -81,7 +95,7 @@
 ):
     tile_size = block_tiles.shape[-1]
     n_rep = lax.axis_size("rep")
-    n_row = lax.axis_size("row")
+    n_row = lax.axis_size("x") * lax.axis_size("z") * lax.axis_size("core")
     fin = features.shape[1]
     fout = weight.shape[1]
     node_total = features.shape[0] * n_row * n_rep
@@ -89,11 +103,11 @@
     slot_count = block_tiles.shape[2] * block_tiles.shape[3]
     tiles = block_tiles.reshape(slot_count, tile_size, tile_size)
     rows = tile_rows.reshape(slot_count)
-    cols = tile_columns.reshape(slot_count)
+    cols = panel_index(tile_columns.reshape(slot_count))
     live = tile_live.reshape(slot_count)
     weight_wide = weight.astype(jnp.float32)
 
-    x_panel = gather_rows_a2a(features.reshape(-1, tile_size, fin), "row")
+    x_panel = gather_rows(features.reshape(-1, tile_size, fin))
     x_panel = x_panel.reshape(n_row, tile_size, fin)
     z_parts = aggregate(tiles, cols, rows, live, [x_panel], group_rows)
     z_own = reduce_rep_a2a(z_parts.reshape(n_rep, -1, fin)).reshape(-1, fin)
@@ -105,7 +119,7 @@
     grad_hidden = pullback(cotangent.astype(jnp.float32))[0]
 
     joined = jnp.concatenate([z_own, grad_hidden], axis=1)
-    joined_all = lax.all_gather(joined, "row", axis=0, tiled=True)
+    joined_all = gather_rows(joined).reshape(-1, joined.shape[1])
     z_quarter = joined_all[:, :fin]
     dh_quarter = joined_all[:, fin:]
     p_quarter = jnp.dot(
@@ -136,15 +150,23 @@
 
 
 def solution(mesh):
+    n_row = mesh.shape["row"]
+    n_core = 2
+    n_z = 8 if n_row % (8 * n_core) == 0 else 1
+    fine = Mesh(
+        mesh.devices.reshape(n_row // (n_z * n_core), n_z, n_core, mesh.shape["rep"]),
+        ("x", "z", "core", "rep"),
+    )
+    row = ("x", "z", "core")
     in_specs = (
-        P(("row", "rep"), None),
+        P((*row, "rep"), None),
         P(),
         P(),
-        P(("row", "rep"), None),
-        P("row", "rep", None, None, None, None),
-        P("row", "rep", None, None),
-        P("row", "rep", None, None),
-        P("row", "rep", None, None),
+        P((*row, "rep"), None),
+        P(row, "rep", None, None, None, None),
+        P(row, "rep", None, None),
+        P(row, "rep", None, None),
+        P(row, "rep", None, None),
     )
-    out_specs = (P(("row", "rep"), None), P(("row", "rep"), None), P(), P())
-    return jax.shard_map(shards, mesh=mesh, in_specs=in_specs, out_specs=out_specs, check_vma=False)
+    out_specs = (P((*row, "rep"), None), P((*row, "rep"), None), P(), P())
+    return jax.shard_map(shards, mesh=fine, in_specs=in_specs, out_specs=out_specs, check_vma=False)

time: 254 us -> 269 us (1.059)
  blocking collectives: 74.7 us -> 95.7 us
  between operations: 14.1 us -> 0.76 us
  starting transfers between devices: 8.91 us -> 18.7 us
  local copies, waits for them, and re-layouts: 2.18 us -> 11.3 us
  matrix products: 18.7 us -> 12.3 us
  other arithmetic: 10.4 us -> 6.71 us
    all_gather x1 -> x0, waiting for transfers between devices: 90 us -> none  [shards(): joined_all = lax.all_gather(joined, 'row', axis=0, tiled=True)]
    all_to_all x0 -> x2, waiting for transfers between devices: none -> 81.2 us  [gather_a2a(): return lax.all_to_all(spread, axis, 0, 0, tiled=False)]
    all_to_all x1 -> x4, blocking collectives: 64.1 us -> 86.3 us  [gather_a2a(): return lax.all_to_all(spread, axis, 0, 0, tiled=False)]
    all_to_all x0 -> x2, starting transfers between devices: none -> 11.8 us  [gather_a2a(): return lax.all_to_all(spread, axis, 0, 0, tiled=False)]
    broadcast_in_dim x1 -> x6, local copies, waits for them, and re-layouts: 1.25 us -> 10.3 us  [gather_a2a(): spread = jnp.broadcast_to(block[None], (n,) + block.shape)]
    all_to_all x2, waiting for transfers between devices: 7.77 us -> 15.9 us  [reduce_rep_a2a(): received = lax.all_to_all(parts, 'rep', 0, 0, tiled=False)]
    dot_general x1, matrix products: 11.5 us -> 7.38 us  [shards(): lax.dot_general(z_quarter, dh_quarter, (((0,), (0,)), ((), ())), precisio...]
    reduce_sum x1, other arithmetic: 4.59 us -> 1.1 us  [shards(): bias_term = jnp.sum(dh_quarter, axis=0)]
  transfers between devices with their start and end apart: 3 -> 4, of which waited for: 2 -> 4; matrix products, arithmetic and copies ran while one was open for 7% -> 0% of each run, Pallas kernels for 0% -> 0%
where the time goes in v2:
time: 269 us; the launch traced here: 266 us
  waiting for transfers between devices  97.1 us (36%)
  blocking collectives  95.7 us (36%)
  Pallas kernels  23.9 us (9%)
  starting transfers between devices  18.7 us (7%)
  matrix products  12.3 us (5%)
  local copies, waits for them, and re-layouts  11.3 us (4%)
  other arithmetic  6.71 us (2%)
    all_to_all x4, blocking collectives, gather_a2a(): return lax.all_to_all(spread, axis, 0, 0, tiled=False)  86.3 us
    all_to_all x2, waiting for transfers between devices, gather_a2a(): return lax.all_to_all(spread, axis, 0, 0, tiled=False)  81.2 us
    pallas_call x2, Pallas kernels, aggregate(): pl.pallas_call(_agg_kernel, grid_spec=grid_spec, out_shape=jax.ShapeDtype...  23.9 us
    all_to_all x2, waiting for transfers between devices, reduce_rep_a2a(): received = lax.all_to_all(parts, 'rep', 0, 0, tiled=False)  15.9 us
    all_to_all x2, starting transfers between devices, gather_a2a(): return lax.all_to_all(spread, axis, 0, 0, tiled=False)  11.8 us
    broadcast_in_dim x6, local copies, waits for them, and re-layouts, gather_a2a(): spread = jnp.broadcast_to(block[None], (n,) + block.shape)  10.3 us
    all_to_all x1, blocking collectives, reduce_rep_a2a(): received = lax.all_to_all(parts, 'rep', 0, 0, tiled=False)  9.4 us
    dot_general x1, matrix products, shards(): lax.dot_general(z_quarter, dh_quarter, (((0,), (0,)), ((), ())), precisio...  7.38 us
  transfers between devices with their start and end apart: 4, of which 4 were waited for; matrix products, arithmetic and copies ran while one was open for 0% of the time, Pallas kernels for 0%

profile of v2, /device:TPU:1, one launch (start us, length us, event | category | flops | bytes accessed | tf_op | source)
XLA Modules:
  0.0 266.3 jit_solution(12127313585142100824)
XLA Ops:
  0.6 0.0 copy-start
  0.6 0.0 copy-start.3
  0.7 0.8 broadcast_in_dim.22
  1.5 19.3 %all_to_all.45 = bf16[8,1,128,128]{3,2,1,0:T(8,128)(2,1)S(1)} all-to-all(bf16[8,1,128,128]{3,2,1,0:T(8,128)(2,1)S(1)} %broadcast_in_dim.22), channel_id=1, replica_groups=mesh['x'=4,'z'=8,'core'=2,'rep'=4] {'z'}, dimensions={0} | all-to-all | bytes 524288 | tf_op jit(solution)/shard_map/all_to_all | solution.py:58
  20.8 1.2 broadcast_in_dim.24
  22.0 4.0 %all-to-all-start.1 = ((bf16[4,8,1,128,128]{4,3,1,2,0:T(8,128)(2,1)}), bf16[4,8,1,128,128]{4,3,1,2,0:T(8,128)(2,1)S(1)}, u32[]{:S(2)}, u32[]{:S(2)}) async-start(bf16[4,8,1,128,128]{4,3,1,2,0:T(8,128)(2,1)} %broadcast_in_dim.24), calls=%async_computation.1 | async-start | bytes 2097152 | tf_op jit(solution)/shard_map/all_to_all | solution.py:58
  26.0 0.0 copy-done.3
  26.0 0.5 fusion.18.cols_ref
  26.5 11.8 %all-to-all-done.1 = bf16[4,8,1,128,128]{4,3,1,2,0:T(8,128)(2,1)S(1)} async-done(((bf16[4,8,1,128,128]{4,3,1,2,0:T(8,128)(2,1)}), bf16[4,8,1,128,128]{4,3,1,2,0:T(8,128)(2,1)S(1)}, u32[]{:S(2)}, u32[]{:S(2)}) %all-to-all-start.1) | async-done | bytes 1048608 | tf_op jit(solution)/shard_map/all_to_all | solution.py:58
  38.3 0.5 broadcast_in_dim.26
  38.8 9.7 %all_to_all.46 = bf16[2,4,8,1,128,128]{5,4,2,1,3,0:T(8,128)(2,1)} all-to-all(bf16[2,4,8,1,128,128]{5,4,2,1,3,0:T(8,128)(2,1)S(1)} %broadcast_in_dim.26), channel_id=1, replica_groups=mesh['x'=4,'z'=8,'core'=2,'rep'=4] {'core'}, dimensions={0} | all-to-all | bytes 4194304 | tf_op jit(solution)/shard_map/all_to_all | solution.py:58
  48.5 0.0 copy-start.1
  48.5 0.0 copy-start.2
  48.5 11.0 %shard_map.111 = f32[4,128,128]{2,1,0:T(8,128)} custom-call(s32[96]{0:T(128)} %fusion.18.cols_ref, s32[96]{0:T(128)} %bitcast.45, s32[96]{0:T(128)} %bitcast.47, bf16[96,128,128]{2,1,0:T(8,128)(2,1)} %bitcast.39, bf16[64,128,128]{2,1,0:T(8,128)(2,1)} %bitcast.41), custom_call_target="tpu_custom_call" | custom-call | tf_op jit(solution)/shard_map/pallas_call | solution.py:47
  59.5 9.4 %all_to_all.47 = f32[4,128,128]{2,1,0:T(8,128)S(1)} all-to-all(f32[4,128,128]{2,1,0:T(8,128)} %shard_map.111), channel_id=1, replica_groups=mesh['x'=4,'z'=8,'core'=2,'rep'=4] {'rep'}, dimensions={0} | all-to-all | bytes 524288 | tf_op jit(solution)/shard_map/all_to_all | solution.py:76
  68.9 0.0 copy-done
  68.9 0.0 copy-done.1
  69.0 0.0 copy-done.2
  69.0 0.9 fusion.6
  69.9 0.1 broadcast_in_dim.27
  70.0 40.1 %all_to_all.48 = f32[8,128,384]{2,1,0:T(8,128)S(1)} all-to-all(f32[8,128,384]{2,1,0:T(8,128)S(1)} %broadcast_in_dim.27), channel_id=1, replica_groups=mesh['x'=4,'z'=8,'core'=2,'rep'=4] {'z'}, dimensions={0} | all-to-all | bytes 3145728 | tf_op jit(solution)/shard_map/all_to_all | solution.py:58
  110.1 3.4 %broadcast_in_dim.28 = f32[4,8,128,384]{3,2,1,0:T(8,128)} broadcast(f32[8,128,384]{2,1,0:T(8,128)S(1)} %all_to_all.48), dimensions={1,2,3} | broadcast | bytes 7864320 | tf_op jit(solution)/shard_map/broadcast_in_dim | solution.py:57
  113.4 7.8 %all-to-all-start.5 = ((f32[4,8,128,384]{3,2,1,0:T(8,128)}), f32[4,8,128,384]{3,2,1,0:T(8,128)}, u32[]{:S(2)}, u32[]{:S(2)}) async-start(f32[4,8,128,384]{3,2,1,0:T(8,128)} %broadcast_in_dim.28), calls=%async_computation.5 | async-start | bytes 12582912 | tf_op jit(solution)/shard_map/all_to_all | solution.py:58
  121.2 0.1 pad.2.clone
  121.3 69.4 %all-to-all-done.5 = f32[4,8,128,384]{3,2,1,0:T(8,128)} async-done(((f32[4,8,128,384]{3,2,1,0:T(8,128)}), f32[4,8,128,384]{3,2,1,0:T(8,128)}, u32[]{:S(2)}, u32[]{:S(2)}) %all-to-all-start.5) | async-done | bytes 6291488 | tf_op jit(solution)/shard_map/all_to_all | solution.py:58
  190.7 4.3 %broadcast_in_dim.29 = f32[2,4,8,128,384]{4,3,2,1,0:T(8,128)S(1)} broadcast(f32[4,8,128,384]{3,2,1,0:T(8,128)} %all-to-all-done.5), dimensions={1,2,3,4} | broadcast | bytes 18874368 | tf_op jit(solution)/shard_map/broadcast_in_dim | solution.py:57
  195.1 17.2 %all_to_all.49 = f32[2,4,8,128,384]{4,3,2,1,0:T(8,128)S(1)} all-to-all(f32[2,4,8,128,384]{4,3,2,1,0:T(8,128)S(1)} %broadcast_in_dim.29), channel_id=1, replica_groups=mesh['x'=4,'z'=8,'core'=2,'rep'=4] {'core'}, dimensions={0} | all-to-all | bytes 25165824 | tf_op jit(solution)/shard_map/all_to_all | solution.py:58
  212.3 4.0 %fusion.2 = f32[8192,128]{1,0:T(8,128)S(1)} fusion(bf16[128,256]{1,0:T(8,128)(2,1)S(1)} %copy-done, f32[8192,384]{1,0:T(8,128)S(1)} %bitcast.35), kind=kOutput, calls=%fused_computation.3 | convolution fusion | flops 3221225472 | bytes 12648448 | tf_op jit(solution)/shard_map/dot_general | solution.py:125
  216.3 1.1 slice_reduce_fusion
  217.4 7.4 %fusion = f32[128,256]{1,0:T(8,128)S(1)} fusion(f32[8192,384]{1,0:T(8,128)S(1)} %bitcast.37), kind=kOutput, calls=%fused_computation.1 | convolution fusion | flops 3221225472 | bytes 12713984 | tf_op jit(solution)/shard_map/dot_general | solution.py:132
  224.8 3.1 %subtract_convert_fusion = (bf16[64,128,128]{2,1,0:T(8,128)(2,1)}, bf16[64,128,128]{2,1,0:T(8,128)(2,1)}) fusion(f32[64,128,128]{2,1,0:T(8,128)S(1)} %bitcast.38), kind=kLoop, calls=%fused_computation.6 | loop fusion | flops 4194304 | bytes 8388608 | tf_op jit(solution)/shard_map/convert_element_type | solution.py:89
  227.9 12.9 %shard_map.112 = f32[4,128,128]{2,1,0:T(8,128)} custom-call(s32[96]{0:T(128)} %fusion.18.cols_ref, s32[96]{0:T(128)} %bitcast.46, s32[96]{0:T(128)} %bitcast.48, bf16[96,128,128]{2,1,0:T(8,128)(2,1)} %bitcast.40, bf16[64,128,128]{2,1,0:T(8,128)(2,1)} %get-tuple-element.5.rest_0_, bf16[64,128,128]{2,1,0:T(8,128)(2,1)} %get-tuple-element.4.rest_1_), custom_call_target="tpu_custom_call" | custom-call | tf_op jit(solution)/shard_map/pallas_call | solution.py:47
  240.7 3.4 %all-to-all-start.7 = ((f32[4,128,128]{2,1,0:T(8,128)}), f32[4,128,128]{2,1,0:T(8,128)S(1)}, u32[]{:S(2)}, u32[]{:S(2)}) async-start(f32[4,128,128]{2,1,0:T(8,128)} %shard_map.112), calls=%async_computation.7 | async-start | bytes 524288 | tf_op jit(solution)/shard_map/all_to_all | solution.py:76
  244.2 0.1 maximum_maximum_fusion
  244.2 7.0 %all-to-all-done.7 = f32[4,128,128]{2,1,0:T(8,128)S(1)} async-done(((f32[4,128,128]{2,1,0:T(8,128)}), f32[4,128,128]{2,1,0:T(8,128)S(1)}, u32[]{:S(2)}, u32[]{:S(2)}) %all-to-all-start.7) | async-done | bytes 262176 | tf_op jit(solution)/shard_map/all_to_all | solution.py:76
  251.3 0.8 broadcast_in_dim.62
  252.1 3.5 %all-to-all-start.8 = ((f32[4,136,256]{2,1,0:T(8,128)}), f32[4,136,256]{2,1,0:T(8,128)S(1)}, u32[]{:S(2)}, u32[]{:S(2)}) async-start(f32[4,136,256]{2,1,0:T(8,128)} %broadcast_in_dim.62), calls=%async_computation.8 | async-start | bytes 1114112 | tf_op jit(solution)/shard_map/all_to_all | solution.py:76
  255.6 0.6 fusion.17
  256.2 8.9 %all-to-all-done.8 = f32[4,136,256]{2,1,0:T(8,128)S(1)} async-done(((f32[4,136,256]{2,1,0:T(8,128)}), f32[4,136,256]{2,1,0:T(8,128)S(1)}, u32[]{:S(2)}, u32[]{:S(2)}) %all-to-all-start.8) | async-done | bytes 557088 | tf_op jit(solution)/shard_map/all_to_all | solution.py:76
  265.1 0.7 fusion.14
  265.8 0.6 slice_multiply_fusion.1
  (4 shorter events, 0.1 us)
Async XLA Ops:
  0.6 68.3 %copy-start = (bf16[128,256]{1,0:T(8,128)(2,1)S(1)}, bf16[128,256]{1,0:T(8,128)(2,1)}, u32[]{:S(2)}) copy-start(bf16[128,256]{1,0:T(8,128)(2,1)} %param.9) | copy-start | bytes 196612
  0.6 25.4 %copy-start.3 = (s32[1,1,96,1]{2,3,1,0:T(1,128)S(1)}, s32[1,1,96,1]{2,3,1,0:T(1,128)}, u32[]{:S(2)}) copy-start(s32[1,1,96,1]{2,3,1,0:T(1,128)} %param.14) | copy-start | bytes 1156
  22.0 16.3 %all-to-all-start.1 = ((bf16[4,8,1,128,128]{4,3,1,2,0:T(8,128)(2,1)}), bf16[4,8,1,128,128]{4,3,1,2,0:T(8,128)(2,1)S(1)}, u32[]{:S(2)}, u32[]{:S(2)}) async-start(bf16[4,8,1,128,128]{4,3,1,2,0:T(8,128)(2,1)} %broadcast_in_dim.24), calls=%async_computation.1 | async-start | bytes 2097152 | tf_op jit(solution)/shard_map/all_to_all | solution.py:58
  48.5 20.5 %copy-start.1 = (bf16[128,256]{1,0:T(8,128)(2,1)S(1)}, bf16[128,256]{1,0:T(8,128)(2,1)}, u32[]{:S(2)}) copy-start(bf16[128,256]{1,0:T(8,128)(2,1)} %param.11) | copy-start | bytes 196612
  48.5 20.5 %copy-start.2 = (f32[256]{0:T(256)S(1)}, f32[256]{0:T(256)}, u32[]{:S(2)}) copy-start(f32[256]{0:T(256)} %param.10) | copy-start | bytes 3076
  113.4 77.3 %all-to-all-start.5 = ((f32[4,8,128,384]{3,2,1,0:T(8,128)}), f32[4,8,128,384]{3,2,1,0:T(8,128)}, u32[]{:S(2)}, u32[]{:S(2)}) async-start(f32[4,8,128,384]{3,2,1,0:T(8,128)} %broadcast_in_dim.28), calls=%async_computation.5 | async-start | bytes 12582912 | tf_op jit(solution)/shard_map/all_to_all | solution.py:58
  240.7 10.5 %all-to-all-start.7 = ((f32[4,128,128]{2,1,0:T(8,128)}), f32[4,128,128]{2,1,0:T(8,128)S(1)}, u32[]{:S(2)}, u32[]{:S(2)}) async-start(f32[4,128,128]{2,1,0:T(8,128)} %shard_map.112), calls=%async_computation.7 | async-start | bytes 524288 | tf_op jit(solution)/shard_map/all_to_all | solution.py:76
  252.1 13.0 %all-to-all-start.8 = ((f32[4,136,256]{2,1,0:T(8,128)}), f32[4,136,256]{2,1,0:T(8,128)S(1)}, u32[]{:S(2)}, u32[]{:S(2)}) async-start(f32[4,136,256]{2,1,0:T(8,128)} %broadcast_in_dim.62), calls=%async_computation.8 | async-start | bytes 1114112 | tf_op jit(solution)/shard_map/all_to_all | solution.py:76
